TPU v7x, 256 devices: a whole 4x4x8 slice. The times are simulated.
256 devices in a mesh: oi: 16 (over y, x_hi, core), oj: 16 (over z, x_lo).
Axes of the slice: x: 4 (x_hi: 2, x_lo: 2; x = x_hi * 2 + x_lo), y: 4, z: 8, core: 2. Of those that a mesh axis runs over, the one named last changes fastest.
Arguments:
- amps: bfloat16 [64, 64, 32768], P('oi', 'oj'), may hold values from -6 to 6
- ladder_w: bfloat16 [2016, 2016], P('oj'), may hold values from -0.125 to 0.125
- fock: bfloat16 [64, 64], replicated, may hold values from -0.75 to 0.75
- eps_occ: float32 [64], replicated, may hold values from -2 to -0.3
- eps_pair: float32 [32768], replicated, may hold values from 0.5 to 4
Outputs:
- update: bfloat16 [64, 64, 32768], P('oi', 'oj')
All inputs are finite; a program needn't handle non-finite values.
Results may differ from a plain program's by a relative error of at most 0.0054.
Values may be sent and summed in bfloat16 or wider, within the bound.
No kernel may reach another device: no remote copies, remote signals or barrier semaphores. Data moves between devices by JAX's collectives and lax.ppermute only.
A program may use at most 128 MiB of HBM per device.

v0:
```python
import jax
import jax.numpy as jnp
import numpy as np
from jax import lax
from jax.sharding import PartitionSpec as P


def pair_tables(occ):
    first, second = np.triu_indices(occ, 1)
    upper = (first * occ + second).astype(np.int32)
    lower = (second * occ + first).astype(np.int32)
    npairs = upper.shape[0]
    expand = np.full((occ * occ,), 2 * npairs, dtype=np.int32)
    expand[upper] = np.arange(npairs, dtype=np.int32)
    expand[lower] = npairs + np.arange(npairs, dtype=np.int32)
    return (upper, lower, expand)


def divide_out(resid, energies, first_eps, second_eps):
    denom = energies[None, None, :] - first_eps[:, None, None] - second_eps[None, :, None]
    held = lax.optimization_barrier(resid)
    return (held.astype(jnp.float32) / denom).astype(jnp.bfloat16)


def on_device(amps, ladder_w, fock, eps_occ, eps_pair):
    pair_amps = lax.all_to_all(
        lax.all_to_all(amps, "oi", split_axis=2, concat_axis=0, tiled=True),
        "oj",
        split_axis=2,
        concat_axis=1,
        tiled=True,
    )
    occ = pair_amps.shape[0]
    width = pair_amps.shape[2]
    upper, lower, expand = pair_tables(occ)
    flat = pair_amps.reshape(occ * occ, width)
    anti = (flat[upper].astype(jnp.float32) - flat[lower].astype(jnp.float32)).astype(jnp.bfloat16)
    contract = (((0,), (0,)), ((), ()))
    whole_w = lax.all_gather(ladder_w, "oj", axis=0, tiled=True)
    ladder = lax.dot_general(
        whole_w, anti[:, 0 : 0 + width], contract, preferred_element_type=jnp.float32
    )
    mixed = jnp.einsum("ikp,kj->ijp", pair_amps, fock, preferred_element_type=jnp.float32)
    filler = jnp.zeros((1, width), jnp.float32)
    full = jnp.concatenate([ladder, -ladder, filler], axis=0)[expand].reshape(occ, occ, width)
    resid = (full - (mixed - jnp.transpose(mixed, (1, 0, 2)))).astype(jnp.bfloat16)
    outgoing = resid.reshape(occ, occ, 1, 1, width)
    landed = lax.all_to_all(
        lax.all_to_all(outgoing, "oi", split_axis=0, concat_axis=2, tiled=True),
        "oj",
        split_axis=1,
        concat_axis=3,
        tiled=True,
    )
    rows_i = landed.shape[0]
    rows_j = landed.shape[1]
    arrived = landed.reshape(rows_i, rows_j, landed.shape[2] * landed.shape[3] * width)
    first_eps = lax.dynamic_slice_in_dim(eps_occ, lax.axis_index("oi") * rows_i, rows_i, 0)
    second_eps = lax.dynamic_slice_in_dim(eps_occ, lax.axis_index("oj") * rows_j, rows_j, 0)
    return divide_out(arrived, eps_pair, first_eps, second_eps)


def solution(mesh):
    in_specs = (P("oi", "oj", None), P("oj", None), P(), P(), P())
    out_specs = P("oi", "oj", None)
    return jax.shard_map(
        on_device, mesh=mesh, in_specs=in_specs, out_specs=out_specs, check_vma=False
    )
```

profile of v0, /device:TPU:2, one launch (start us, length us, event | category | flops | bytes accessed | tf_op | source)
XLA Modules:
  0.0 460.0 jit_solution(2015257166413810704)
XLA Ops:
  6.5 0.0 copy-start
  6.5 0.0 all-gather.3.cloned.1.call-start
  6.5 0.7 all-gather.3.cloned.1.call-update
  7.3 34.8 %copy.33 = bf16[4,4,32768]{1,0,2:T(4,128)(2,1)} copy(bf16[4,4,32768]{2,1,0:T(4,128)(2,1)} %param.11) | data formatting | bytes 2097152 | tf_op args[0]
  42.1 67.7 %reshape.75 = bf16[16,2,16384]{2,1,0:T(2,128)(2,1)S(1)} reshape(bf16[32768,4,4]{2,1,0:T(4,128)(2,1)} %bitcast.50) | data formatting | bytes 2097152
  109.8 48.0 %all_to_all.69 = bf16[16,2,16384]{2,1,0:T(2,128)(2,1)S(1)} all-to-all(bf16[16,2,16384]{2,1,0:T(2,128)(2,1)S(1)} %reshape.75), channel_id=1, replica_groups=mesh['oi'=16,'oj'=16] {'oi'}, dimensions={0} | all-to-all | bytes 2097152 | tf_op jit(solution)/shard_map/all_to_all | solution.py:27
  157.7 73.1 %reshape.76 = bf16[32768,4,4]{2,1,0:T(4,128)(2,1)} reshape(bf16[16,2,16384]{2,1,0:T(2,128)(2,1)S(1)} %all_to_all.69) | data formatting | bytes 2097152
  230.8 47.0 %copy.34 = bf16[4,4,16,2048]{3,1,0,2:T(4,128)(2,1)S(1)} copy(bf16[4,4,16,2048]{1,0,3,2:T(4,128)(2,1)} %bitcast.49) | data formatting | bytes 2097152 | tf_op jit(solution)/shard_map/all_to_all | solution.py:27
  277.8 1.7 copy.35
  279.5 0.0 copy-start.4
  279.5 0.0 copy-start.3
  279.5 0.0 copy-start.2
  279.5 2.2 reshape.77
  281.8 8.8 %all-to-all-start.1 = ((bf16[16,2,16384]{2,1,0:T(2,128)(2,1)}), bf16[16,2,16384]{2,1,0:T(2,128)(2,1)S(1)}, u32[]{:S(2)}, u32[]{:S(2)}) async-start(bf16[16,2,16384]{2,1,0:T(2,128)(2,1)} %reshape.77), calls=%async_computation.1 | async-start | bytes 2097152 | tf_op jit(solution)/shard_map/all_to_all | solution.py:26
  290.6 0.1 pad.2.clone
  290.7 0.0 copy-done.4
  290.7 0.0 copy-done.3
  290.7 0.0 copy-done.2
  290.7 27.0 %all-to-all-done.1 = bf16[16,2,16384]{2,1,0:T(2,128)(2,1)S(1)} async-done(((bf16[16,2,16384]{2,1,0:T(2,128)(2,1)}), bf16[16,2,16384]{2,1,0:T(2,128)(2,1)S(1)}, u32[]{:S(2)}, u32[]{:S(2)}) %all-to-all-start.1) | async-done | bytes 1048608 | tf_op jit(solution)/shard_map/all_to_all | solution.py:26
  317.7 1.3 reshape.78
  319.1 1.4 copy.36
  320.5 6.3 %gather_fusion.1 = bf16[2016,128]{1,0:T(8,128)(2,1)S(1)} fusion(bf16[4096,128]{1,0:T(8,128)(2,1)S(1)} %bitcast.51, s32[2048]{0:T(1024)S(1)} %pad_clamp_fusion), kind=kCustom, calls=%fused_computation.1 | custom fusion | bytes 1040256 | tf_op jit(solution)/shard_map/gather | solution.py:37
  326.8 6.3 %gather_fusion = bf16[2016,128]{1,0:T(8,128)(2,1)S(1)} fusion(bf16[4096,128]{1,0:T(8,128)(2,1)S(1)} %bitcast.52, s32[2048]{0:T(1024)S(1)} %pad_clamp_fusion.1), kind=kCustom, calls=%fused_computation | custom fusion | bytes 1040256 | tf_op jit(solution)/shard_map/gather | solution.py:37
  333.1 0.0 copy-done
  333.2 1.8 fusion.4
  335.0 0.0 all-gather.3.cloned.1.call-done
  335.0 14.1 %copy.37 = bf16[16,126,2016]{1,0,2:T(8,128)(2,1)} copy(bf16[16,126,2016]{1,2,0:T(8,128)(2,1)} %all-gather.3.cloned.1.call-done) | data formatting | bytes 16257024 | tf_op jit(solution)/shard_map/all_gather | solution.py:39
  349.1 15.7 %reshape.72 = bf16[2016,2016]{0,1:T(8,128)(2,1)} reshape(bf16[16,126,2016]{1,0,2:T(8,128)(2,1)} %copy.37) | data formatting | bytes 16257024
  364.8 5.7 %fusion.7 = (f32[2016,128]{1,0:T(8,128)S(1)}, f32[2016,128]{1,0:T(8,128)S(1)}) fusion(bf16[2016,2016]{0,1:T(8,128)(2,1)} %reshape.72, bf16[2016,128]{1,0:T(8,128)(2,1)S(1)} %gather_fusion.1, bf16[2016,128]{1,0:T(8,128)(2,1)S(1)} %gather_fusion), kind=kOutput, calls=%fused_computation.20 | convolution fusion | flops 1041739776 | bytes 11225088 | tf_op jit(solution)/shard_map/dot_general | solution.py:40
  370.6 3.1 maximum_maximum_fusion
  373.7 14.2 %gather_fusion.2 = f32[4096,128]{1,0:T(8,128)} fusion(f32[4033,128]{1,0:T(8,128)S(1)} %maximum_maximum_fusion, s32[4096]{0:T(1024)S(1)} %broadcast_clamp_fusion), kind=kCustom, calls=%fused_computation.2 | custom fusion | bytes 4210688 | tf_op jit(solution)/shard_map/gather | solution.py:45
  387.8 5.2 %fusion.3 = bf16[64,64,1,1,128]{4,0,1,3,2:T(8,128)(2,1)S(1)} fusion(f32[64,64,128]{2,0,1:T(8,128)} %fusion.4, f32[64,64,128]{2,1,0:T(8,128)} %bitcast.56), kind=kLoop, calls=%fused_computation.10 | loop fusion | flops 1572864 | bytes 5242880 | tf_op jit(solution)/shard_map/reshape | solution.py:47
  393.1 0.0 copy-start.5
  393.1 1.6 copy.41
  394.7 3.7 all-to-all-start.2
  398.4 0.0 copy-done.5
  398.4 0.1 fusion.6
  398.5 17.9 %all-to-all-done.2 = bf16[64,64,1,1,128]{4,1,3,2,0:T(8,128)(2,1)S(1)} async-done(((bf16[64,64,1,1,128]{4,1,3,2,0:T(8,128)(2,1)}), bf16[64,64,1,1,128]{4,1,3,2,0:T(8,128)(2,1)S(1)}, u32[]{:S(2)}, u32[]{:S(2)}) %all-to-all-start.2) | async-done | bytes 1048608 | tf_op jit(solution)/shard_map/all_to_all | solution.py:49
  416.4 0.0 copy-start.1
  416.4 1.8 copy.53
  418.2 4.9 %all-to-all-start.3 = ((bf16[4,64,16,1,128]{4,0,2,3,1:T(4,128)(2,1)}), bf16[4,64,16,1,128]{4,0,2,3,1:T(4,128)(2,1)S(1)}, u32[]{:S(2)}, u32[]{:S(2)}) async-start(bf16[4,64,16,1,128]{4,0,2,3,1:T(4,128)(2,1)} %bitcast.48), calls=%async_computation.3 | async-start | bytes 2097152 | tf_op jit(solution)/shard_map/all_to_all | solution.py:48
  423.1 0.0 copy-done.1
  423.1 0.2 broadcast_subtract_fusion
  423.2 27.1 %all-to-all-done.3 = bf16[4,64,16,1,128]{4,0,2,3,1:T(4,128)(2,1)S(1)} async-done(((bf16[4,64,16,1,128]{4,0,2,3,1:T(4,128)(2,1)}), bf16[4,64,16,1,128]{4,0,2,3,1:T(4,128)(2,1)S(1)}, u32[]{:S(2)}, u32[]{:S(2)}) %all-to-all-start.3) | async-done | bytes 1048608 | tf_op jit(solution)/shard_map/all_to_all | solution.py:48
  450.3 0.7 copy.43
  451.0 0.4 reshape.46
  451.4 1.8 fusion.2
  (3 shorter events, 0.0 us)
Async XLA Ops:
  6.5 326.6 %copy-start = (bf16[64,64]{1,0:T(8,128)(2,1)S(1)}, bf16[64,64]{1,0:T(8,128)(2,1)}, u32[]{:S(2)}) copy-start(bf16[64,64]{1,0:T(8,128)(2,1)} %param.13) | copy-start | bytes 24580
  6.5 328.4 %all-gather.3.cloned.1.call-start = ((), (), s32[]{:S(2)}) async-start(), calls=%async_computation.4 | async-start | bytes 8773632 | tf_op jit(solution)/shard_map/all_gather | solution.py:39
  279.5 11.2 %copy-start.4 = (s32[2016]{0:T(1024)S(1)}, s32[2016]{0:T(1024)}, u32[]{:S(2)}) copy-start(s32[2016]{0:T(1024)} %constant.39) | copy-start | bytes 24196
  279.5 11.2 %copy-start.3 = (s32[2016]{0:T(1024)S(1)}, s32[2016]{0:T(1024)}, u32[]{:S(2)}) copy-start(s32[2016]{0:T(1024)} %constant.38) | copy-start | bytes 24196
  279.5 11.2 %copy-start.2 = (s32[4096]{0:T(1024)S(1)}, s32[4096]{0:T(1024)}, u32[]{:S(2)}) copy-start(s32[4096]{0:T(1024)} %constant.40) | copy-start | bytes 49156
  281.8 36.0 %all-to-all-start.1 = ((bf16[16,2,16384]{2,1,0:T(2,128)(2,1)}), bf16[16,2,16384]{2,1,0:T(2,128)(2,1)S(1)}, u32[]{:S(2)}, u32[]{:S(2)}) async-start(bf16[16,2,16384]{2,1,0:T(2,128)(2,1)} %reshape.77), calls=%async_computation.1 | async-start | bytes 2097152 | tf_op jit(solution)/shard_map/all_to_all | solution.py:26
  393.1 5.3 %copy-start.5 = (f32[64]{0:T(128)S(1)}, f32[64]{0:T(128)}, u32[]{:S(2)}) copy-start(f32[64]{0:T(128)} %param.14) | copy-start | bytes 772
  394.7 21.7 %all-to-all-start.2 = ((bf16[64,64,1,1,128]{4,1,3,2,0:T(8,128)(2,1)}), bf16[64,64,1,1,128]{4,1,3,2,0:T(8,128)(2,1)S(1)}, u32[]{:S(2)}, u32[]{:S(2)}) async-start(bf16[64,64,1,1,128]{4,1,3,2,0:T(8,128)(2,1)} %copy.41), calls=%async_computation.2 | async-start | bytes 2097152 | tf_op jit(solution)/shard_map/all_to_all | solution.py:49
  416.4 6.7 %copy-start.1 = (f32[32768]{0:T(1024)S(1)}, f32[32768]{0:T(1024)}, u32[]{:S(2)}) copy-start(f32[32768]{0:T(1024)} %param.15) | copy-start | bytes 393220
  418.2 32.1 %all-to-all-start.3 = ((bf16[4,64,16,1,128]{4,0,2,3,1:T(4,128)(2,1)}), bf16[4,64,16,1,128]{4,0,2,3,1:T(4,128)(2,1)S(1)}, u32[]{:S(2)}, u32[]{:S(2)}) async-start(bf16[4,64,16,1,128]{4,0,2,3,1:T(4,128)(2,1)} %bitcast.48), calls=%async_computation.3 | async-start | bytes 2097152 | tf_op jit(solution)/shard_map/all_to_all | solution.py:48
Sparse Core Ops, SparseCore 0:
  9.1 192.8 all-gather.2
where the time goes:
time: 465 us; the launch traced here: 460 us
  local copies, waits for them, and re-layouts  291 us (63%)
  waiting for transfers between devices  72.7 us (16%)
  blocking collectives  48 us (10%)
  starting transfers between devices  17.4 us (4%)
  between operations  13.6 us (3%)
  other arithmetic  10.3 us (2%)
  matrix products  7.52 us (2%)
    unnamed x18, local copies, waits for them, and re-layouts  195 us
    all_to_all x2, local copies, waits for them, and re-layouts, on_device(): lax.all_to_all(amps, 'oi', split_axis=2, concat_axis=0, tiled=True)  48.7 us
    all_to_all x1, blocking collectives, on_device(): lax.all_to_all(amps, 'oi', split_axis=2, concat_axis=0, tiled=True)  48 us
    all_to_all x1, waiting for transfers between devices, on_device(): lax.all_to_all(lax.all_to_all(outgoing, 'oi', split_axis=0, concat_axis=2...  27.1 us
    all_to_all x1, waiting for transfers between devices, on_device(): lax.all_to_all(lax.all_to_all(amps, 'oi', split_axis=2, concat_axis=0, ti...  27 us
    all_to_all x1, waiting for transfers between devices, on_device(): lax.all_to_all(outgoing, 'oi', split_axis=0, concat_axis=2, tiled=True)  17.9 us
    gather x1, local copies, waits for them, and re-layouts, on_device(): jnp.concatenate([ladder, -ladder, filler], axis=0)[expand]  14.2 us
    all_gather x1, local copies, waits for them, and re-layouts, on_device(): whole_w = lax.all_gather(ladder_w, 'oj', axis=0, tiled=True)  14.1 us
  transfers between devices with their start and end apart: 4, of which 3 were waited for; matrix products, arithmetic and copies ran while one was open for 53% of the time, Pallas kernels for 0%

commit v1 on v0

--- a/solution.py
+++ b/solution.py
@@ -36,7 +36,9 @@
     flat = pair_amps.reshape(occ * occ, width)
     anti = (flat[upper].astype(jnp.float32) - flat[lower].astype(jnp.float32)).astype(jnp.bfloat16)
     contract = (((0,), (0,)), ((), ()))
-    whole_w = lax.all_gather(ladder_w, "oj", axis=0, tiled=True)
+    whole_w = jnp.concatenate(
+        lax.all_to_all(jnp.stack([ladder_w] * lax.axis_size("oj")), "oj", 0, 0), axis=0
+    )
     ladder = lax.dot_general(
         whole_w, anti[:, 0 : 0 + width], contract, preferred_element_type=jnp.float32
     )

time: 465 us -> 608 us (1.31)
  waiting for transfers between devices: 72.7 us -> 212 us
  between operations: 13.6 us -> 0.18 us
  blocking collectives: 48 us -> 60 us
    all_to_all x1, waiting for transfers between devices: 27 us -> 168 us  [on_device(): lax.all_to_all(jnp.stack([ladder_w] * lax.axis_size('oj')), 'oj', 0, 0)]
    all_to_all x0 -> x1, blocking collectives: none -> 36.1 us  [on_device(): lax.all_to_all(lax.all_to_all(amps, 'oi', split_axis=2, concat_axis=0, ti...]
    all_to_all x1, blocking collectives: 48 us -> 23.9 us  [on_device(): lax.all_to_all(amps, 'oi', split_axis=2, concat_axis=0, tiled=True)]
    unnamed x18 -> x19, local copies, waits for them, and re-layouts: 195 us -> 178 us
    reshape x0 -> x1, local copies, waits for them, and re-layouts: none -> 15.7 us  [on_device(): jnp.concatenate(lax.all_to_all(jnp.stack([ladder_w] * lax.axis_size('oj')...]
    all_gather x1 -> x0, local copies, waits for them, and re-layouts: 14.1 us -> none  [on_device(): whole_w = lax.all_gather(ladder_w, 'oj', axis=0, tiled=True)]
    all_to_all x0 -> x1, local copies, waits for them, and re-layouts: none -> 14.1 us  [on_device(): lax.all_to_all(jnp.stack([ladder_w] * lax.axis_size('oj')), 'oj', 0, 0)]
  transfers between devices with their start and end apart: 4 -> 3, of which waited for: 3 -> 3; matrix products, arithmetic and copies ran while one was open for 53% -> 3% of each run, Pallas kernels for 0% -> 0%
where the time goes in v1:
time: 608 us; the launch traced here: 602 us
  local copies, waits for them, and re-layouts  294 us (48%)
  waiting for transfers between devices  212 us (35%)
  blocking collectives  60 us (10%)
  starting transfers between devices  18.1 us (3%)
  other arithmetic  10.3 us (2%)
  matrix products  7.53 us (1%)
    unnamed x19, local copies, waits for them, and re-layouts  178 us
    all_to_all x1, waiting for transfers between devices, on_device(): lax.all_to_all(jnp.stack([ladder_w] * lax.axis_size('oj')), 'oj', 0, 0)  168 us
    all_to_all x2, local copies, waits for them, and re-layouts, on_device(): lax.all_to_all(amps, 'oi', split_axis=2, concat_axis=0, tiled=True)  48.7 us
    all_to_all x1, blocking collectives, on_device(): lax.all_to_all(lax.all_to_all(amps, 'oi', split_axis=2, concat_axis=0, ti...  36.1 us
    all_to_all x1, waiting for transfers between devices, on_device(): lax.all_to_all(lax.all_to_all(outgoing, 'oi', split_axis=0, concat_axis=2...  26.8 us
    all_to_all x1, blocking collectives, on_device(): lax.all_to_all(amps, 'oi', split_axis=2, concat_axis=0, tiled=True)  23.9 us
    all_to_all x1, waiting for transfers between devices, on_device(): lax.all_to_all(outgoing, 'oi', split_axis=0, concat_axis=2, tiled=True)  17.9 us
    reshape x1, local copies, waits for them, and re-layouts, on_device(): jnp.concatenate(lax.all_to_all(jnp.stack([ladder_w] * lax.axis_size('oj')...  15.7 us
  transfers between devices with their start and end apart: 3, of which 3 were waited for; matrix products, arithmetic and copies ran while one was open for 3% of the time, Pallas kernels for 0%

profile of v1, /device:TPU:2, one launch (start us, length us, event | category | flops | bytes accessed | tf_op | source)
XLA Modules:
  0.0 602.5 jit_solution(1943676671823965468)
XLA Ops:
  0.0 0.0 copy-start
  0.0 34.8 %copy.33 = bf16[4,4,32768]{1,0,2:T(4,128)(2,1)} copy(bf16[4,4,32768]{2,1,0:T(4,128)(2,1)} %param.11) | data formatting | bytes 2097152 | tf_op args[0]
  34.8 67.6 %reshape.79 = bf16[16,2,16384]{2,1,0:T(2,128)(2,1)S(1)} reshape(bf16[32768,4,4]{2,1,0:T(4,128)(2,1)} %bitcast.49) | data formatting | bytes 2097152
  102.5 23.9 %all_to_all.74 = bf16[16,2,16384]{2,1,0:T(2,128)(2,1)S(1)} all-to-all(bf16[16,2,16384]{2,1,0:T(2,128)(2,1)S(1)} %reshape.79), channel_id=1, replica_groups=mesh['oi'=16,'oj'=16] {'oi'}, dimensions={0} | all-to-all | bytes 2097152 | tf_op jit(solution)/shard_map/all_to_all | solution.py:27
  126.4 73.1 %reshape.80 = bf16[32768,4,4]{2,1,0:T(4,128)(2,1)} reshape(bf16[16,2,16384]{2,1,0:T(2,128)(2,1)S(1)} %all_to_all.74) | data formatting | bytes 2097152
  199.4 47.0 %copy.34 = bf16[4,4,16,2048]{3,1,0,2:T(4,128)(2,1)S(1)} copy(bf16[4,4,16,2048]{1,0,3,2:T(4,128)(2,1)} %bitcast.48) | data formatting | bytes 2097152 | tf_op jit(solution)/shard_map/all_to_all | solution.py:27
  246.4 1.7 copy.35
  248.1 1.5 reshape.81
  249.6 0.0 copy-start.1
  249.6 36.1 %all_to_all.75 = bf16[16,2,16384]{2,1,0:T(2,128)(2,1)S(1)} all-to-all(bf16[16,2,16384]{2,1,0:T(2,128)(2,1)S(1)} %reshape.81), channel_id=1, replica_groups=mesh['oi'=16,'oj'=16] {'oj'}, dimensions={0} | all-to-all | bytes 2097152 | tf_op jit(solution)/shard_map/all_to_all | solution.py:26
  285.7 0.0 copy-done.1
  285.7 4.2 stack.2
  289.9 0.0 copy-start.5
  289.9 0.0 copy-start.4
  289.9 0.0 copy-start.3
  289.9 6.3 %all-to-all-start.2 = ((bf16[16,126,2016]{1,2,0:T(8,128)(2,1)}), bf16[16,126,2016]{1,2,0:T(8,128)(2,1)}, u32[]{:S(2)}, u32[]{:S(2)}) async-start(bf16[16,126,2016]{1,2,0:T(8,128)(2,1)} %stack.2), calls=%async_computation.2 | async-start | bytes 16515072 | tf_op jit(solution)/shard_map/all_to_all | solution.py:40
  296.3 0.1 pad.2.clone
  296.3 0.0 copy-done.5
  296.4 0.0 copy-done.4
  296.4 0.0 copy-done.3
  296.4 1.3 reshape.82
  297.8 1.4 copy.36
  299.1 6.3 %gather_fusion.1 = bf16[2016,128]{1,0:T(8,128)(2,1)S(1)} fusion(bf16[4096,128]{1,0:T(8,128)(2,1)S(1)} %bitcast.50, s32[2048]{0:T(1024)S(1)} %pad_clamp_fusion), kind=kCustom, calls=%fused_computation.1 | custom fusion | bytes 1040256 | tf_op jit(solution)/shard_map/gather | solution.py:37
  305.5 6.3 %gather_fusion = bf16[2016,128]{1,0:T(8,128)(2,1)S(1)} fusion(bf16[4096,128]{1,0:T(8,128)(2,1)S(1)} %bitcast.51, s32[2048]{0:T(1024)S(1)} %pad_clamp_fusion.1), kind=kCustom, calls=%fused_computation | custom fusion | bytes 1040256 | tf_op jit(solution)/shard_map/gather | solution.py:37
  311.8 0.0 copy-done
  311.9 1.8 fusion.4
  313.7 167.7 %all-to-all-done.2 = bf16[16,126,2016]{1,2,0:T(8,128)(2,1)} async-done(((bf16[16,126,2016]{1,2,0:T(8,128)(2,1)}), bf16[16,126,2016]{1,2,0:T(8,128)(2,1)}, u32[]{:S(2)}, u32[]{:S(2)}) %all-to-all-start.2) | async-done | bytes 8128544 | tf_op jit(solution)/shard_map/all_to_all | solution.py:40
  481.3 14.1 %copy.37 = bf16[16,126,2016]{1,0,2:T(8,128)(2,1)} copy(bf16[16,126,2016]{1,2,0:T(8,128)(2,1)} %all-to-all-done.2) | data formatting | bytes 16257024 | tf_op jit(solution)/shard_map/all_to_all | solution.py:40
  495.4 15.7 %reshape.49 = bf16[2016,2016]{0,1:T(8,128)(2,1)} reshape(bf16[16,126,2016]{1,0,2:T(8,128)(2,1)} %copy.37) | data formatting | bytes 16257024 | tf_op jit(solution)/shard_map/reshape | solution.py:39
  511.2 5.7 fusion.7
  516.9 3.1 maximum_maximum_fusion
  520.0 14.2 %gather_fusion.2 = f32[4096,128]{1,0:T(8,128)} fusion(f32[4033,128]{1,0:T(8,128)S(1)} %maximum_maximum_fusion, s32[4096]{0:T(1024)S(1)} %broadcast_clamp_fusion), kind=kCustom, calls=%fused_computation.2 | custom fusion | bytes 4210688 | tf_op jit(solution)/shard_map/gather | solution.py:47
  534.2 5.2 fusion.3
  539.4 0.0 copy-start.6
  539.4 1.6 copy.41
  541.1 3.9 all-to-all-start.3
  545.0 0.0 copy-done.6
  545.0 0.1 fusion.6
  545.1 17.9 %all-to-all-done.3 = bf16[64,64,1,1,128]{4,1,3,2,0:T(8,128)(2,1)S(1)} async-done(((bf16[64,64,1,1,128]{4,1,3,2,0:T(8,128)(2,1)}), bf16[64,64,1,1,128]{4,1,3,2,0:T(8,128)(2,1)S(1)}, u32[]{:S(2)}, u32[]{:S(2)}) %all-to-all-start.3) | async-done | bytes 1048608 | tf_op jit(solution)/shard_map/all_to_all | solution.py:51
  563.0 0.0 copy-start.2
  563.0 1.8 copy.53
  564.8 7.9 %all-to-all-start.4 = ((bf16[4,64,16,1,128]{4,0,2,3,1:T(4,128)(2,1)}), bf16[4,64,16,1,128]{4,0,2,3,1:T(4,128)(2,1)S(1)}, u32[]{:S(2)}, u32[]{:S(2)}) async-start(bf16[4,64,16,1,128]{4,0,2,3,1:T(4,128)(2,1)} %bitcast.47), calls=%async_computation.4 | async-start | bytes 2097152 | tf_op jit(solution)/shard_map/all_to_all | solution.py:50
  572.7 0.0 copy-done.2
  572.7 0.2 broadcast_subtract_fusion
  572.8 26.8 %all-to-all-done.4 = bf16[4,64,16,1,128]{4,0,2,3,1:T(4,128)(2,1)S(1)} async-done(((bf16[4,64,16,1,128]{4,0,2,3,1:T(4,128)(2,1)}), bf16[4,64,16,1,128]{4,0,2,3,1:T(4,128)(2,1)S(1)}, u32[]{:S(2)}, u32[]{:S(2)}) %all-to-all-start.4) | async-done | bytes 1048608 | tf_op jit(solution)/shard_map/all_to_all | solution.py:50
  599.6 0.7 copy.43
  600.3 0.4 reshape.52
  600.7 1.8 fusion.2
  (3 shorter events, 0.0 us)
Async XLA Ops:
  0.0 311.8 %copy-start = (bf16[64,64]{1,0:T(8,128)(2,1)S(1)}, bf16[64,64]{1,0:T(8,128)(2,1)}, u32[]{:S(2)}) copy-start(bf16[64,64]{1,0:T(8,128)(2,1)} %param.13) | copy-start | bytes 24580
  249.6 36.1 %copy-start.1 = (bf16[126,2016]{0,1:T(8,128)(2,1)S(1)}, bf16[126,2016]{0,1:T(8,128)(2,1)}, u32[]{:S(2)}) copy-start(bf16[126,2016]{0,1:T(8,128)(2,1)} %param.12) | copy-start | bytes 1524100
  289.9 6.4 %copy-start.5 = (s32[2016]{0:T(1024)S(1)}, s32[2016]{0:T(1024)}, u32[]{:S(2)}) copy-start(s32[2016]{0:T(1024)} %constant.39) | copy-start | bytes 24196
  289.9 6.4 %copy-start.4 = (s32[2016]{0:T(1024)S(1)}, s32[2016]{0:T(1024)}, u32[]{:S(2)}) copy-start(s32[2016]{0:T(1024)} %constant.38) | copy-start | bytes 24196
  289.9 6.5 %copy-start.3 = (s32[4096]{0:T(1024)S(1)}, s32[4096]{0:T(1024)}, u32[]{:S(2)}) copy-start(s32[4096]{0:T(1024)} %constant.40) | copy-start | bytes 49156
  289.9 191.4 %all-to-all-start.2 = ((bf16[16,126,2016]{1,2,0:T(8,128)(2,1)}), bf16[16,126,2016]{1,2,0:T(8,128)(2,1)}, u32[]{:S(2)}, u32[]{:S(2)}) async-start(bf16[16,126,2016]{1,2,0:T(8,128)(2,1)} %stack.2), calls=%async_computation.2 | async-start | bytes 16515072 | tf_op jit(solution)/shard_map/all_to_all | solution.py:40
  539.4 5.6 copy-start.6
  541.1 22.0 %all-to-all-start.3 = ((bf16[64,64,1,1,128]{4,1,3,2,0:T(8,128)(2,1)}), bf16[64,64,1,1,128]{4,1,3,2,0:T(8,128)(2,1)S(1)}, u32[]{:S(2)}, u32[]{:S(2)}) async-start(bf16[64,64,1,1,128]{4,1,3,2,0:T(8,128)(2,1)} %copy.41), calls=%async_computation.3 | async-start | bytes 2097152 | tf_op jit(solution)/shard_map/all_to_all | solution.py:51
  563.0 9.7 %copy-start.2 = (f32[32768]{0:T(1024)S(1)}, f32[32768]{0:T(1024)}, u32[]{:S(2)}) copy-start(f32[32768]{0:T(1024)} %param.15) | copy-start | bytes 393220
  564.8 34.8 %all-to-all-start.4 = ((bf16[4,64,16,1,128]{4,0,2,3,1:T(4,128)(2,1)}), bf16[4,64,16,1,128]{4,0,2,3,1:T(4,128)(2,1)S(1)}, u32[]{:S(2)}, u32[]{:S(2)}) async-start(bf16[4,64,16,1,128]{4,0,2,3,1:T(4,128)(2,1)} %bitcast.47), calls=%async_computation.4 | async-start | bytes 2097152 | tf_op jit(solution)/shard_map/all_to_all | solution.py:50
